TPU v7x, 256 devices: a whole 4x4x8 slice. The times are simulated.
256 devices in a mesh: dp: 4 (over x), ctx: 16 (over z, y_hi), tp: 4 (over y_lo, core).
Axes of the slice: x: 4, y: 4 (y_hi: 2, y_lo: 2; y = y_hi * 2 + y_lo), z: 8, core: 2. Of those that a mesh axis runs over, the one named last changes fastest.
Arguments:
- query_rows: bfloat16 [16384, 4096], P(('dp', 'ctx'), 'tp'), parts along dimension 0, may hold values from -6 to 6
- key_matrix: bfloat16 [16384, 512], P(('dp', 'ctx'), 'tp'), parts along dimension 0, may hold values from -6 to 6
- value_matrix: bfloat16 [16384, 512], P(('dp', 'ctx'), 'tp'), parts along dimension 0, may hold values from -6 to 6
- attn_out: bfloat16 [16384, 4096], P(('dp', 'ctx'), 'tp'), parts along dimension 0, may hold values from -6 to 6
- out_grad: bfloat16 [16384, 4096], P(('dp', 'ctx', 'tp')), parts along dimension 0, may hold values from -0.5 to 0.5
- log_sums: float32 [32, 16384], P('tp', ('dp', 'ctx')), parts along dimension 1, may hold values from 3 to 5
- block_mask: int32 [128, 32], P('dp'), parts along dimension 0, may hold values 0 or 1
Outputs:
- query_grad: bfloat16 [16384, 4096], P(('dp', 'ctx'), 'tp'), parts along dimension 0
- key_gradient: bfloat16 [16384, 512], P(('dp', 'ctx'), 'tp'), parts along dimension 0
- value_gradient: bfloat16 [16384, 512], P(('dp', 'ctx'), 'tp'), parts along dimension 0
There are 4 independent parts, one for each index of `dp`. A program takes and returns all parts, laid end to end along the dimension named above; each array names one. Nothing has to cross between parts.
Inputs may be any that keep to these rules, and one draw needn't show every extreme that they name: `block_mask`: entry [a, b] with b < a lets query block a see key block b; entries on and above the diagonal are never read.
All inputs are finite; a program needn't handle non-finite values.
Results may differ from a plain program's by a relative error of at most 0.0049.
Values may be sent and summed in bfloat16 or wider, within the bound.
No kernel may reach another device: no remote copies, remote signals or barrier semaphores. Data moves between devices by JAX's collectives and lax.ppermute only.
A program may use at most 64 MiB of HBM per device.

v0:
```python
import math
import jax
import jax.numpy as jnp
from jax import lax
from jax.sharding import PartitionSpec as P

BLK = 128
HEAD_SIZE = 128


def live_region(block_mask, query_start, tok_rows, key_start, key_count):
    block_table = lax.dynamic_slice(
        block_mask, (query_start // BLK, key_start // BLK), (tok_rows // BLK, key_count // BLK)
    )
    block_table = jnp.repeat(jnp.repeat(block_table, BLK, axis=0), BLK, axis=1)
    query_pos = query_start + jnp.arange(tok_rows, dtype=jnp.int32)
    key_pos = key_start + jnp.arange(key_count, dtype=jnp.int32)
    query_block = (query_pos // BLK)[:, None]
    key_block = (key_pos // BLK)[None, :]
    earlier = (key_block < query_block) & (block_table == 1)
    diagonal = (key_block == query_block) & (key_pos[None, :] <= query_pos[:, None])
    return earlier | diagonal


def contract(queries, out_grads, row_delta, log_sums, keys_part, values_part, live_mask):
    logit_scale = 1.0 / math.sqrt(HEAD_SIZE)
    scores = (
        jnp.einsum("igd,jd->gij", queries, keys_part, preferred_element_type=jnp.float32)
        * logit_scale
    )
    probabilities = jnp.where(live_mask[None], jnp.exp(scores - log_sums[:, :, None]), 0.0)
    prob_grad = jnp.einsum(
        "igd,jd->gij", out_grads, values_part, preferred_element_type=jnp.float32
    )
    dscore = (probabilities * (prob_grad - row_delta[:, :, None])).astype(jnp.bfloat16)
    query_term = jnp.einsum("gij,jd->igd", dscore, keys_part, preferred_element_type=jnp.float32)
    key_term = jnp.einsum("gij,igd->jd", dscore, queries, preferred_element_type=jnp.float32)
    value_term = jnp.einsum(
        "gij,igd->jd",
        probabilities.astype(jnp.bfloat16),
        out_grads,
        preferred_element_type=jnp.float32,
    )
    return (query_term, key_term, value_term)


def local(query_rows, key_matrix, value_matrix, attn_out, out_grad, log_sums, block_mask):
    tok_rows = query_rows.shape[0]
    col_width = query_rows.shape[1]
    heads_local = col_width // HEAD_SIZE
    ctx_pos = lax.axis_index("ctx")
    ctx_count = lax.axis_size("ctx")
    tp_count = lax.axis_size("tp")
    grad_rows = out_grad.shape[0]
    pieces = out_grad.reshape(grad_rows, tp_count, col_width)
    own_grad = lax.all_to_all(pieces, "tp", split_axis=1, concat_axis=0, tiled=True)
    own_grad = own_grad.reshape(tok_rows, col_width)
    queries = query_rows.reshape(tok_rows, heads_local, HEAD_SIZE)
    out_grads = own_grad.reshape(tok_rows, heads_local, HEAD_SIZE)
    outputs = attn_out.reshape(tok_rows, heads_local, HEAD_SIZE)
    row_delta = jnp.sum(out_grads.astype(jnp.float32) * outputs.astype(jnp.float32), axis=2).T
    query_start = ctx_pos * tok_rows
    key_values = jnp.concatenate([key_matrix, value_matrix], axis=1)
    all_key_values = lax.all_gather(key_values, "ctx", axis=0, tiled=True)
    zero_query = jnp.zeros((tok_rows, heads_local, HEAD_SIZE), jnp.float32)
    zero_partial = jnp.zeros((ctx_count * tok_rows, 2 * HEAD_SIZE), jnp.float32)

    def visit_span(span, carried):
        query_acc, partial = carried
        key_start = span * tok_rows
        span_kv = lax.dynamic_slice_in_dim(all_key_values, key_start, tok_rows, 0)
        keys_part = span_kv[:, :HEAD_SIZE]
        values_part = span_kv[:, HEAD_SIZE:]
        live_mask = live_region(block_mask, query_start, tok_rows, key_start, tok_rows)
        query_term, key_term, value_term = contract(
            queries, out_grads, row_delta, log_sums, keys_part, values_part, live_mask
        )
        span_partial = jnp.concatenate([key_term, value_term], axis=1)
        partial = lax.dynamic_update_slice_in_dim(partial, span_partial, key_start, 0)
        return (query_acc + query_term, partial)

    query_acc, partial = lax.fori_loop(0, ctx_pos + 1, visit_span, (zero_query, zero_partial))
    summed = lax.psum_scatter(partial, "ctx", scatter_dimension=0, tiled=True)
    logit_scale = 1.0 / math.sqrt(HEAD_SIZE)
    query_grad = (query_acc * logit_scale).reshape(tok_rows, col_width).astype(jnp.bfloat16)
    key_gradient = (summed[:, :HEAD_SIZE] * logit_scale).astype(jnp.bfloat16)
    value_gradient = summed[:, HEAD_SIZE:].astype(jnp.bfloat16)
    return (query_grad, key_gradient, value_gradient)


def solution(mesh):
    placed = (
        P(("dp", "ctx"), "tp"),
        P(("dp", "ctx"), "tp"),
        P(("dp", "ctx"), "tp"),
        P(("dp", "ctx"), "tp"),
        P(("dp", "ctx", "tp"), None),
        P("tp", ("dp", "ctx")),
        P("dp", None),
    )
    return jax.shard_map(
        local,
        mesh=mesh,
        in_specs=placed,
        out_specs=(P(("dp", "ctx"), "tp"), P(("dp", "ctx"), "tp"), P(("dp", "ctx"), "tp")),
        check_vma=False,
    )
```

profile of v0, /device:TPU:4, one launch (start us, length us, event | category | flops | bytes accessed | tf_op | source)
XLA Modules:
  0.0 429.3 jit_solution(2428679739724852573)
XLA Ops:
  7.2 0.0 copy-start.1
  7.2 0.0 copy-start
  7.2 0.0 all-gather.2.cloned.1.call-start
  7.2 1.6 pad_maximum_fusion.1
  8.8 0.0 all-gather.2.cloned.1.call-update
  8.9 1.9 copy.66
  10.7 3.5 all-to-all-start
  14.2 0.0 reduce-scatter.2.cloned.1.call-start
  14.3 0.0 copy-done.1
  14.3 0.2 copy.40
  14.5 0.0 copy-done
  14.5 0.1 convert_bitcast_fusion
  14.6 0.2 copy.62
  14.8 8.2 %all-to-all-done = bf16[64,4,1024]{2,0,1:T(8,128)(2,1)S(1)} async-done(((bf16[64,4,1024]{2,0,1:T(8,128)(2,1)}), bf16[64,4,1024]{2,0,1:T(8,128)(2,1)S(1)}, u32[]{:S(2)}, u32[]{:S(2)}) %all-to-all-start) | async-done | bytes 524320 | tf_op jit(solution)/shard_map/all_to_all | solution.py:56
  23.0 0.1 copy.61
  23.1 0.3 copy.43
  23.5 0.3 multiply_reduce_fusion
  23.8 0.1 copy.44
  23.9 75.2 %all-gather.2.cloned.1.call-done = bf16[4096,256]{1,0:T(8,128)(2,1)} async-done(((bf16[256,256]{1,0:T(8,128)(2,1)}), bf16[4096,256]{1,0:T(8,128)(2,1)}) %all-gather.2.cloned.1.call-update) | async-done | bytes 2097168 | tf_op jit(solution)/shard_map/all_gather | solution.py:64
  99.1 0.1 broadcast_in_dim.48
  99.2 0.0 copy-start.2
  99.2 2.2 broadcast_in_dim.49.clone
  101.4 0.0 copy-done.2
  101.4 6.9 %while.15 = (s32[]{:T(128)}, f32[256,8,128]{0,2,1:T(8,128)S(1)}, f32[4096,256]{1,0:T(8,128)}, s32[]{:T(128)}, bf16[4096,256]{1,0:T(8,128)(2,1)}, /*index=5*/s32[...) while((s32[]{:T(128)}, f32[256,8,128]{0,2,1:T(8,128)S(1)}, ...), condition=%wide.region_2.3_spmd, body=%wide.region_1.2_spmd.sunk | while | flops 675487744 | bytes 15821342 | solution.py:82
  101.4 0.8 dynamic_slice.15
  102.2 0.1 copy.70
  102.3 0.1 broadcast_bitcast_fusion.2
  102.4 0.2 fusion.34
  102.6 1.4 fusion.35
  104.0 0.5 convolution_bitcast_fusion.5
  104.5 1.3 fusion.36
  105.7 0.5 convolution_bitcast_fusion.6
  106.2 1.2 fusion.37
  107.5 0.1 copy.72
  107.6 0.7 constant_dynamic-update-slice_fusion.2
  108.3 0.0 reduce-scatter.2.cloned.1.call-update
  108.3 0.1 multiply_convert_fusion
  108.4 1.0 copy.54
  109.4 309.9 %reduce-scatter.2.cloned.1.call-done = f32[256,256]{1,0:T(8,128)} async-done(((f32[4096,256]{1,0:T(8,128)}), f32[256,256]{1,0:T(8,128)}) %reduce-scatter.2.cloned.1.call-update) | async-done | bytes 262160 | tf_op jit(solution)/shard_map/reduce_scatter | solution.py:83
  419.3 1.5 slice.29
  420.9 1.5 fusion.9
  (5 shorter events, 0.1 us)
Async XLA Ops:
  7.2 7.1 %copy-start.1 = (bf16[256,1024]{1,0:T(8,128)(2,1)S(1)}, bf16[256,1024]{1,0:T(8,128)(2,1)}, u32[]{:S(2)}) copy-start(bf16[256,1024]{1,0:T(8,128)(2,1)} %param.9) | copy-start | bytes 1572868
  7.2 7.3 %copy-start = (bf16[256,1024]{1,0:T(8,128)(2,1)S(1)}, bf16[256,1024]{1,0:T(8,128)(2,1)}, u32[]{:S(2)}) copy-start(bf16[256,1024]{1,0:T(8,128)(2,1)} %param.12) | copy-start | bytes 1572868
  7.2 91.9 %all-gather.2.cloned.1.call-start = ((), (), s32[]{:S(2)}) async-start(), calls=%async_computation.2 | async-start | bytes 2228224 | tf_op jit(solution)/shard_map/all_gather | solution.py:64
  10.7 12.3 %all-to-all-start = ((bf16[64,4,1024]{2,0,1:T(8,128)(2,1)}), bf16[64,4,1024]{2,0,1:T(8,128)(2,1)S(1)}, u32[]{:S(2)}, u32[]{:S(2)}) async-start(bf16[64,4,1024]{2,0,1:T(8,128)(2,1)} %bitcast.62), calls=%async_computation | async-start | bytes 1048576 | tf_op jit(solution)/shard_map/all_to_all | solution.py:56
  14.2 405.1 %reduce-scatter.2.cloned.1.call-start = ((), (), s32[]{:S(2)}) async-start(), calls=%async_computation.3 | async-start | bytes 4456448 | tf_op jit(solution)/shard_map/reduce_scatter | solution.py:83
  99.2 2.2 copy-start.2
Sparse Core Ops, SparseCore 0:
  10.6 88.4 all-gather.1
  108.5 310.8 reduce-scatter.1
where the time goes:
time: 432 us; the launch traced here: 429 us
  waiting for transfers between devices  393 us (91%)
  between operations  14.2 us (3%)
  local copies, waits for them, and re-layouts  9.4 us (2%)
  matrix products  4.83 us (1%)
    reduce_scatter x1, waiting for transfers between devices, local(): summed = lax.psum_scatter(partial, 'ctx', scatter_dimension=0, tiled=True)  310 us
    all_gather x1, waiting for transfers between devices, local(): all_key_values = lax.all_gather(key_values, 'ctx', axis=0, tiled=True)  75.2 us
  transfers between devices with their start and end apart: 3, of which 3 were waited for; matrix products, arithmetic and copies ran while one was open for 1% of the time, Pallas kernels for 0%

commit v1 on v0

--- a/solution.py
+++ b/solution.py
@@ -3,6 +3,7 @@
 import jax.numpy as jnp
 from jax import lax
 from jax.sharding import PartitionSpec as P
+from jax.lax import all_to_all, axis_size
 
 BLK = 128
 HEAD_SIZE = 128
@@ -61,7 +62,10 @@
     row_delta = jnp.sum(out_grads.astype(jnp.float32) * outputs.astype(jnp.float32), axis=2).T
     query_start = ctx_pos * tok_rows
     key_values = jnp.concatenate([key_matrix, value_matrix], axis=1)
-    all_key_values = lax.all_gather(key_values, "ctx", axis=0, tiled=True)
+    met_up = axis_size("ctx")
+    seen_now = jnp.stack([key_values] * met_up, 0)
+    y1 = all_to_all(seen_now, axis_name="ctx", split_axis=0, concat_axis=0)
+    all_key_values = jnp.concatenate(y1, 0)
     zero_query = jnp.zeros((tok_rows, heads_local, HEAD_SIZE), jnp.float32)
     zero_partial = jnp.zeros((ctx_count * tok_rows, 2 * HEAD_SIZE), jnp.float32)
 

time: 432 us -> 417 us (0.965)
  waiting for transfers between devices: 393 us -> 367 us
  starting transfers between devices: 3.55 us -> 14.9 us
    all_gather x1 -> x0, waiting for transfers between devices: 75.2 us -> none  [local(): all_key_values = lax.all_gather(key_values, 'ctx', axis=0, tiled=True)]
    all_to_all x0 -> x1, waiting for transfers between devices: none -> 50.4 us  [local(): y1 = all_to_all(seen_now, axis_name='ctx', split_axis=0, concat_axis=0)]
    all_to_all x0 -> x1, starting transfers between devices: none -> 11.4 us  [local(): y1 = all_to_all(seen_now, axis_name='ctx', split_axis=0, concat_axis=0)]
where the time goes in v1:
time: 417 us; the launch traced here: 414 us
  waiting for transfers between devices  367 us (88%)
  starting transfers between devices  14.9 us (4%)
  between operations  14.2 us (3%)
  local copies, waits for them, and re-layouts  11 us (3%)
  matrix products  4.83 us (1%)
    reduce_scatter x1, waiting for transfers between devices, local(): summed = lax.psum_scatter(partial, 'ctx', scatter_dimension=0, tiled=True)  308 us
    all_to_all x1, waiting for transfers between devices, local(): y1 = all_to_all(seen_now, axis_name='ctx', split_axis=0, concat_axis=0)  50.4 us
    all_to_all x1, starting transfers between devices, local(): y1 = all_to_all(seen_now, axis_name='ctx', split_axis=0, concat_axis=0)  11.4 us
    all_to_all x1, waiting for transfers between devices, local(): lax.all_to_all(pieces, 'tp', split_axis=1, concat_axis=0, tiled=True)  8.77 us
  transfers between devices with their start and end apart: 3, of which 3 were waited for; matrix products, arithmetic and copies ran while one was open for 1% of the time, Pallas kernels for 0%

profile of v1, /device:TPU:4, one launch (start us, length us, event | category | flops | bytes accessed | tf_op | source)
XLA Modules:
  0.0 414.2 jit_solution(5802424766093783550)
XLA Ops:
  7.2 0.0 copy-start.2
  7.2 0.0 copy-start.3
  7.2 1.9 copy.66
  9.1 3.5 all-to-all-start.1
  12.6 0.0 copy-done.2
  12.6 0.0 copy-done.3
  12.6 8.8 %all-to-all-done.1 = bf16[64,4,1024]{2,0,1:T(8,128)(2,1)S(1)} async-done(((bf16[64,4,1024]{2,0,1:T(8,128)(2,1)}), bf16[64,4,1024]{2,0,1:T(8,128)(2,1)S(1)}, u32[]{:S(2)}, u32[]{:S(2)}) %all-to-all-start.1) | async-done | bytes 524320 | tf_op jit(solution)/shard_map/all_to_all | solution.py:57
  21.4 1.5 stack.2
  22.9 0.0 copy-start.1
  22.9 0.0 copy-start
  22.9 11.4 %all-to-all-start = ((bf16[16,256,256]{2,1,0:T(8,128)(2,1)}), bf16[16,256,256]{2,1,0:T(8,128)(2,1)}, u32[]{:S(2)}, u32[]{:S(2)}) async-start(bf16[16,256,256]{2,1,0:T(8,128)(2,1)} %stack.2), calls=%async_computation | async-start | bytes 4194304 | tf_op jit(solution)/shard_map/all_to_all | solution.py:67
  34.3 0.0 reduce-scatter.2.cloned.1.call-start
  34.4 0.0 copy-done.1
  34.4 0.2 copy.40
  34.6 0.0 copy-done
  34.6 0.1 convert_bitcast_fusion
  34.7 0.2 copy.62
  34.9 0.1 copy.61
  35.0 0.3 copy.43
  35.4 0.3 multiply_reduce_fusion
  35.7 0.1 copy.44
  35.8 50.4 %all-to-all-done = bf16[16,256,256]{2,1,0:T(8,128)(2,1)} async-done(((bf16[16,256,256]{2,1,0:T(8,128)(2,1)}), bf16[16,256,256]{2,1,0:T(8,128)(2,1)}, u32[]{:S(2)}, u32[]{:S(2)}) %all-to-all-start) | async-done | bytes 2097184 | tf_op jit(solution)/shard_map/all_to_all | solution.py:67
  86.2 0.1 broadcast_in_dim.48
  86.2 0.0 copy-start.4
  86.3 2.2 broadcast_in_dim.49.clone
  88.5 0.0 copy-done.4
  88.5 6.9 %while.15 = (s32[]{:T(128)}, f32[256,8,128]{0,2,1:T(8,128)S(1)}, f32[4096,256]{1,0:T(8,128)}, s32[]{:T(128)}, bf16[4096,256]{1,0:T(8,128)(2,1)}, /*index=5*/s32[...) while((s32[]{:T(128)}, f32[256,8,128]{0,2,1:T(8,128)S(1)}, ...), condition=%wide.region_2.3_spmd, body=%wide.region_1.2_spmd.sunk | while | flops 675487744 | bytes 15821342 | solution.py:86
  88.5 0.8 dynamic_slice.15
  89.3 0.1 copy.70
  89.4 0.1 broadcast_bitcast_fusion.2
  89.5 0.2 fusion.34
  89.6 1.4 fusion.35
  91.1 0.5 convolution_bitcast_fusion.5
  91.5 1.3 fusion.36
  92.8 0.5 convolution_bitcast_fusion.6
  93.3 1.2 fusion.37
  94.5 0.1 copy.72
  94.7 0.7 constant_dynamic-update-slice_fusion.2
  95.4 0.0 reduce-scatter.2.cloned.1.call-update
  95.4 0.1 multiply_convert_fusion
  95.5 1.0 copy.54
  96.5 307.7 %reduce-scatter.2.cloned.1.call-done = f32[256,256]{1,0:T(8,128)} async-done(((f32[4096,256]{1,0:T(8,128)}), f32[256,256]{1,0:T(8,128)}) %reduce-scatter.2.cloned.1.call-update) | async-done | bytes 262160 | tf_op jit(solution)/shard_map/reduce_scatter | solution.py:87
  404.2 1.5 slice.29
  405.8 1.5 fusion.9
  (6 shorter events, 0.1 us)
Async XLA Ops:
  7.2 5.4 %copy-start.2 = (bf16[256,128]{1,0:T(8,128)(2,1)S(1)}, bf16[256,128]{1,0:T(8,128)(2,1)}, u32[]{:S(2)}) copy-start(bf16[256,128]{1,0:T(8,128)(2,1)} %param.11) | copy-start | bytes 196612
  7.2 5.4 %copy-start.3 = (bf16[256,128]{1,0:T(8,128)(2,1)S(1)}, bf16[256,128]{1,0:T(8,128)(2,1)}, u32[]{:S(2)}) copy-start(bf16[256,128]{1,0:T(8,128)(2,1)} %param.10) | copy-start | bytes 196612
  9.1 12.3 %all-to-all-start.1 = ((bf16[64,4,1024]{2,0,1:T(8,128)(2,1)}), bf16[64,4,1024]{2,0,1:T(8,128)(2,1)S(1)}, u32[]{:S(2)}, u32[]{:S(2)}) async-start(bf16[64,4,1024]{2,0,1:T(8,128)(2,1)} %bitcast.63), calls=%async_computation.1 | async-start | bytes 1048576 | tf_op jit(solution)/shard_map/all_to_all | solution.py:57
  22.9 11.5 %copy-start.1 = (bf16[256,1024]{1,0:T(8,128)(2,1)S(1)}, bf16[256,1024]{1,0:T(8,128)(2,1)}, u32[]{:S(2)}) copy-start(bf16[256,1024]{1,0:T(8,128)(2,1)} %param.9) | copy-start | bytes 1572868
  22.9 11.7 %copy-start = (bf16[256,1024]{1,0:T(8,128)(2,1)S(1)}, bf16[256,1024]{1,0:T(8,128)(2,1)}, u32[]{:S(2)}) copy-start(bf16[256,1024]{1,0:T(8,128)(2,1)} %param.12) | copy-start | bytes 1572868
  22.9 63.2 %all-to-all-start = ((bf16[16,256,256]{2,1,0:T(8,128)(2,1)}), bf16[16,256,256]{2,1,0:T(8,128)(2,1)}, u32[]{:S(2)}, u32[]{:S(2)}) async-start(bf16[16,256,256]{2,1,0:T(8,128)(2,1)} %stack.2), calls=%async_computation | async-start | bytes 4194304 | tf_op jit(solution)/shard_map/all_to_all | solution.py:67
  34.3 369.9 %reduce-scatter.2.cloned.1.call-start = ((), (), s32[]{:S(2)}) async-start(), calls=%async_computation.3 | async-start | bytes 4456448 | tf_op jit(solution)/shard_map/reduce_scatter | solution.py:87
  86.2 2.2 copy-start.4
Sparse Core Ops, SparseCore 0:
  95.5 308.6 reduce-scatter.1
